TPU v7x, 32 devices: a whole 2x2x4 slice. The times are simulated.
32 devices in a mesh: shard: 4 (over z), rep: 8 (over y, x, core).
Axes of the slice: x: 2, y: 2, z: 4, core: 2. Of those that a mesh axis runs over, the one named last changes fastest.
Arguments:
- grads: bfloat16 [1, 8192, 28672], P(None, 'shard', 'rep'), may hold values from -81 to 81
- seeds: int32 [1], replicated, may hold values from 0 to 999999
Outputs:
- projected: bfloat16 [512, 1, 28672], P('shard', None, 'rep')
All inputs are finite; a program needn't handle non-finite values.
Results may differ from a plain program's by a relative error of at most 0.0056.
Values may be sent and summed in bfloat16 or wider, within the bound.
No kernel may reach another device: no remote copies, remote signals or barrier semaphores. Data moves between devices by JAX's collectives and lax.ppermute only.
A program may use at most 128 MiB of HBM per device.

v0:
```python
import jax
import jax.numpy as jnp
from jax import lax
from jax.sharding import PartitionSpec as P

RANK = 512
mix_first = 668265263
mix_second = -2048144789
mix_third = -1028477387


def sketch_table(seeds, first_row, count, rank):
    rows = first_row + lax.iota(jnp.int32, count)
    columns = lax.iota(jnp.int32, rank)
    counter = rows[:, None] * jnp.int32(rank) + columns[None, :]
    hashed = jnp.bitwise_xor(counter[None, :, :], (seeds * jnp.int32(mix_first))[:, None, None])
    hashed = hashed * jnp.int32(mix_second)
    hashed = jnp.bitwise_xor(hashed, lax.shift_right_logical(hashed, jnp.int32(15)))
    hashed = hashed * jnp.int32(mix_third)
    hashed = jnp.bitwise_xor(hashed, lax.shift_right_logical(hashed, jnp.int32(13)))
    unit = lax.shift_right_logical(hashed, jnp.int32(8)).astype(jnp.float32) * (1.0 / 16777216.0)
    return (2.0 * unit - 1.0).astype(jnp.bfloat16)


def body(grads, seeds):
    mats, depth, width = grads.shape
    rows_whole = lax.all_to_all(grads, "rep", split_axis=1, concat_axis=2, tiled=True)
    block = rows_whole.shape[2] // 8

    def add_block(step, total):
        start = step * block
        table = sketch_table(seeds, start, block, RANK)
        piece = lax.dynamic_slice_in_dim(rows_whole, start, block, 2)
        return total + jnp.einsum("mdc,mcr->dmr", piece, table, preferred_element_type=jnp.float32)

    sketch_rows = lax.fori_loop(
        0, 8, add_block, jnp.zeros((rows_whole.shape[1], mats, RANK), jnp.float32)
    )
    local_gram = jnp.einsum(
        "dmr,dms->mrs",
        sketch_rows,
        sketch_rows,
        precision=lax.Precision.HIGHEST,
        preferred_element_type=jnp.float32,
    )
    gram = lax.psum(local_gram, ("shard", "rep"))
    factor = jnp.linalg.cholesky(gram)
    own_rows = jnp.transpose(sketch_rows, (1, 0, 2))
    basis_rows = lax.linalg.triangular_solve(
        factor, own_rows, left_side=False, lower=True, transpose_a=True
    ).astype(jnp.bfloat16)
    partial_sum = jnp.einsum(
        "mdr,mdc->rmc",
        lax.all_gather(basis_rows, "rep", axis=1, tiled=True),
        grads,
        preferred_element_type=jnp.float32,
    )
    projected = lax.psum_scatter(partial_sum, "shard", scatter_dimension=0, tiled=True)
    return projected.astype(jnp.bfloat16)


def solution(mesh):
    return jax.shard_map(
        body,
        mesh=mesh,
        in_specs=(P(None, "shard", "rep"), P()),
        out_specs=P("shard", None, "rep"),
        check_vma=False,
    )
```

profile of v0, /device:TPU:0, one launch (start us, length us, event | category | flops | bytes accessed | tf_op | source)
XLA Modules:
  0.0 861.6 jit_solution(14677463218900408071)
XLA Ops:
  6.5 26.0 %copy.30 = bf16[1,2048,3584]{2,0,1:T(2,128)(2,1)} copy(bf16[1,2048,3584]{2,1,0:T(8,128)(2,1)} %param.4) | data formatting | bytes 29360128 | tf_op args[0]
  33.1 94.1 %reduce.36 = bf16[2048,3584]{1,0:T(8,128)(2,1)} reduce(bf16[2048,1,3584]{2,1,0:T(2,128)(2,1)} %bitcast.210, bf16[]{:T(256)} %broadcast.502), dimensions={1}, to_apply=%bitcast.195.reduce_sub_computation | reduce | bytes 29360130
  127.2 16.3 %reshape.459 = bf16[8,2,458752]{2,1,0:T(2,128)(2,1)} reshape(bf16[2048,3584]{1,0:T(8,128)(2,1)} %reduce.36) | data formatting | bytes 29360128
  143.5 5.6 all-to-all-start
  149.9 161.3 %all-to-all-done = bf16[8,2,458752]{2,1,0:T(2,128)(2,1)} async-done(((bf16[8,2,458752]{2,1,0:T(2,128)(2,1)}), bf16[8,2,458752]{2,1,0:T(2,128)(2,1)}, u32[]{:S(2)}, u32[]{:S(2)}) %all-to-all-start) | async-done | bytes 14680096 | tf_op jit(solution)/shard_map/all_to_all | solution.py:27
  311.2 20.2 %reshape.460 = bf16[2048,1,3584]{2,1,0:T(2,128)(2,1)} reshape(bf16[8,2,458752]{2,1,0:T(2,128)(2,1)} %all-to-all-done) | data formatting | bytes 29360128
  331.4 19.4 %copy.28 = bf16[1,2048,3584]{2,1,0:T(8,128)(2,1)} copy(bf16[1,2048,3584]{2,0,1:T(2,128)(2,1)} %bitcast.211) | data formatting | bytes 29360128
  350.8 18.7 %copy.21 = bf16[1,256,8,3584]{1,3,2,0:T(8,128)(2,1)} copy(bf16[1,256,8,3584]{3,1,2,0:T(8,128)(2,1)} %bitcast.212) | data formatting | bytes 29360128 | tf_op jit(solution)/shard_map/all_to_all | solution.py:27
  369.5 42.8 %while.18 = (s32[]{:T(128)}, f32[256,1,512]{0,2,1:T(8,128)S(1)}, s32[1]{0:T(128)}, bf16[1,256,28672]{1,2,0:T(8,128)(2,1)}, s32[]{:T(128)}, /*index=5*/s32[]{:T(128)}, s32[]{:T(128)}, s32[]{:T(128)}) while((s32[]{:T(128)}, f32[256,1,512]{0,2,1:T(8,128)S(1)}, s32[1]{0:T(128)}, bf16[1,256,28672]{1,2,0:T(8,128)(2,1)}, s32[]{:T(128)}, ...), condition=%wide.region_1.0_spmd.clone, body=%wide.region_0.0_spmd.clone.sunk | while | flops 963648512 | bytes 2912917 | solution.py:36
  380.2 5.3 fusion.77
  390.9 5.3 fusion.77
  414.9 130.6 %all-reduce.3.cloned.1.call-done = f32[1,512,512]{1,2,0:T(8,128)} async-done(((f32[1,512,512]{1,2,0:T(8,128)}), f32[1,512,512]{1,2,0:T(8,128)}) %all-reduce.3.cloned.1.call-update) | async-done | bytes 1048592 | tf_op jit(solution)/shard_map/psum | solution.py:46
  548.5 11.7 %custom-call.34 = f32[1,128,128]{2,1,0:T(8,128)S(1)} custom-call(f32[1,128,128]{2,1,0:T(8,128)S(1)} %cholesky.267), custom_call_target="Cholesky" | custom-call | tf_op jit(solution)/shard_map/jit(cholesky)/cholesky | solution.py:47
  560.3 9.8 %custom-call.35 = f32[1,1,128,128]{2,3,1,0:T(8,128)S(1)} custom-call(f32[1,1,128,128]{3,2,1,0:T(8,128)S(1)} %get-tuple-element.173), custom_call_target="InvertDiagBlocksLowerTriangular" | custom-call | tf_op jit(solution)/shard_map/jit(cholesky)/cholesky | solution.py:47
  570.9 11.7 %custom-call.36 = f32[1,128,128]{2,1,0:T(8,128)S(1)} custom-call(f32[1,128,128]{2,1,0:T(8,128)S(1)} %cholesky.271), custom_call_target="Cholesky" | custom-call | tf_op jit(solution)/shard_map/jit(cholesky)/cholesky | solution.py:47
  582.6 10.2 %custom-call.37 = f32[1,1,128,128]{2,3,1,0:T(8,128)S(1)} custom-call(f32[1,1,128,128]{3,2,1,0:T(8,128)S(1)} %get-tuple-element.170), custom_call_target="InvertDiagBlocksLowerTriangular" | custom-call | tf_op jit(solution)/shard_map/jit(cholesky)/cholesky | solution.py:47
  593.5 11.7 %custom-call.38 = f32[1,128,128]{2,1,0:T(8,128)S(1)} custom-call(f32[1,128,128]{2,1,0:T(8,128)S(1)} %cholesky.276), custom_call_target="Cholesky" | custom-call | tf_op jit(solution)/shard_map/jit(cholesky)/cholesky | solution.py:47
  606.0 9.8 %custom-call.39 = f32[1,1,128,128]{2,3,1,0:T(8,128)S(1)} custom-call(f32[1,1,128,128]{3,2,1,0:T(8,128)S(1)} %get-tuple-element.167), custom_call_target="InvertDiagBlocksLowerTriangular" | custom-call | tf_op jit(solution)/shard_map/jit(cholesky)/cholesky | solution.py:47
  616.4 11.7 %custom-call.40 = f32[1,128,128]{2,1,0:T(8,128)S(1)} custom-call(f32[1,128,128]{2,1,0:T(8,128)S(1)} %fusion.46), custom_call_target="Cholesky" | custom-call | tf_op jit(solution)/shard_map/jit(cholesky)/cholesky | solution.py:47
  632.3 8.1 while.17
  640.4 39.3 %custom-call.41 = f32[1,4,128,128]{2,3,1,0:T(8,128)S(1)} custom-call(f32[1,4,128,128]{3,2,1,0:T(8,128)S(1)} %bitcast.221), custom_call_target="InvertDiagBlocksLowerTriangular" | custom-call | tf_op jit(solution)/shard_map/triangular_solve | solution.py:49
  683.7 27.2 %all-gather.2.cloned.1.call-done = bf16[1,2048,512]{1,2,0:T(8,128)(2,1)} async-done(((bf16[1,256,512]{1,2,0:T(8,128)(2,1)}), bf16[1,2048,512]{1,2,0:T(8,128)(2,1)}) %all-gather.2.cloned.1.call-update) | async-done | bytes 2097168 | tf_op jit(solution)/shard_map/all_gather | solution.py:54
  710.9 13.5 %fusion.31 = f32[512,1,3584]{2,0,1:T(8,128)} fusion(bf16[1,2048,3584]{2,1,0:T(8,128)(2,1)} %param.4, bf16[1,2048,512]{1,2,0:T(8,128)(2,1)} %all-gather.2.cloned.1.call-done), kind=kOutput, calls=%fused_computation.27 | convolution fusion | flops 7516192768 | bytes 24117248 | tf_op jit(solution)/shard_map/mdr,mdc->rmc/dot_general | solution.py:52
  724.4 127.9 %reduce-scatter.2.cloned.1.call-done = f32[128,1,3584]{2,0,1:T(8,128)} async-done(((f32[512,1,3584]{2,0,1:T(8,128)}), f32[128,1,3584]{2,0,1:T(8,128)}) %reduce-scatter.2.cloned.1.call-update) | async-done | bytes 1835024 | tf_op jit(solution)/shard_map/reduce_scatter | solution.py:58
  (68 shorter events, 57.1 us)
Async XLA Ops:
  143.5 167.7 %all-to-all-start = ((bf16[8,2,458752]{2,1,0:T(2,128)(2,1)}), bf16[8,2,458752]{2,1,0:T(2,128)(2,1)}, u32[]{:S(2)}, u32[]{:S(2)}) async-start(bf16[8,2,458752]{2,1,0:T(2,128)(2,1)} %reshape.459), calls=%async_computation | async-start | bytes 29360128 | tf_op jit(solution)/shard_map/all_to_all | solution.py:27
  149.1 396.4 %all-reduce.3.cloned.1.call-start = ((), (), s32[]{:S(2)}) async-start(), calls=%async_computation.2 | async-start | bytes 2097152 | tf_op jit(solution)/shard_map/psum | solution.py:46
  414.4 296.5 %all-gather.2.cloned.1.call-start = ((), (), s32[]{:S(2)}) async-start(), calls=%async_computation.3 | async-start | bytes 2359296 | tf_op jit(solution)/shard_map/all_gather | solution.py:54
  683.6 168.7 %reduce-scatter.2.cloned.1.call-start = ((), (), s32[]{:S(2)}) async-start(), calls=%async_computation.4 | async-start | bytes 9175040 | tf_op jit(solution)/shard_map/reduce_scatter | solution.py:58
Sparse Core Ops, SparseCore 0:
  414.5 130.9 all-reduce.2
  683.8 27.0 all-gather.1
  724.5 127.7 reduce-scatter.1
where the time goes:
time: 869 us; the launch traced here: 862 us
  waiting for transfers between devices  447 us (51%)
  other arithmetic  217 us (25%)
  local copies, waits for them, and re-layouts  111 us (13%)
  matrix products  63 us (7%)
  between operations  16.7 us (2%)
    all_to_all x1, waiting for transfers between devices, body(): lax.all_to_all(grads, 'rep', split_axis=1, concat_axis=2, tiled=True)  161 us
    psum x1, waiting for transfers between devices, body(): gram = lax.psum(local_gram, ('shard', 'rep'))  131 us
    reduce_scatter x1, waiting for transfers between devices, body(): lax.psum_scatter(partial_sum, 'shard', scatter_dimension=0, tiled=True)  128 us
    unnamed x3, other arithmetic  94.1 us
    unnamed x5, local copies, waits for them, and re-layouts  82.4 us
    another operation x14, other arithmetic, body(): factor = jnp.linalg.cholesky(gram)  79 us
    dot_general x8, matrix products, add_block(): jnp.einsum('mdc,mcr->dmr', piece, table, preferred_element_type=jnp.float32)  42.5 us
    another operation x4, other arithmetic, body(): lax.linalg.triangular_solve(factor, own_rows, left_side=False, lower=True...  40.2 us
  transfers between devices with their start and end apart: 4, of which 4 were waited for; matrix products, arithmetic and copies ran while one was open for 0% of the time, Pallas kernels for 0%

commit v1 on v0

--- a/solution.py
+++ b/solution.py
@@ -7,6 +7,22 @@
 mix_first = 668265263
 mix_second = -2048144789
 mix_third = -1028477387
+
+
+def ring_product(x, axis, dim, contribution):
+    size, index, extent = (lax.axis_size(axis), lax.axis_index(axis), x.shape[dim])
+    upward = [(i, (i + 1) % size) for i in range(size)]
+    backward = [(i, (i - 1) % size) for i in range(size)]
+    middle = size // 2
+    from_left = from_right = x
+    total = contribution(x, index * extent)
+    for step in range(1, middle + 1):
+        from_left = lax.ppermute(from_left, axis, upward)
+        if step < size - middle:
+            from_right = lax.ppermute(from_right, axis, backward)
+            total = total + contribution(from_right, (index + step) % size * extent)
+        total = total + contribution(from_left, (index - step) % size * extent)
+    return total
 
 
 def sketch_table(seeds, first_row, count, rank):
@@ -49,11 +65,16 @@
     basis_rows = lax.linalg.triangular_solve(
         factor, own_rows, left_side=False, lower=True, transpose_a=True
     ).astype(jnp.bfloat16)
-    partial_sum = jnp.einsum(
-        "mdr,mdc->rmc",
-        lax.all_gather(basis_rows, "rep", axis=1, tiled=True),
-        grads,
-        preferred_element_type=jnp.float32,
+    partial_sum = ring_product(
+        basis_rows,
+        "rep",
+        1,
+        lambda own_block, start_2: jnp.einsum(
+            "mdr,mdc->rmc",
+            own_block,
+            lax.dynamic_slice_in_dim(grads, start_2, own_block.shape[1], axis=1),
+            preferred_element_type=jnp.float32,
+        ),
     )
     projected = lax.psum_scatter(partial_sum, "shard", scatter_dimension=0, tiled=True)
     return projected.astype(jnp.bfloat16)

time: 869 us -> 896 us (1.031)
  matrix products: 63 us -> 106 us
  waiting for transfers between devices: 447 us -> 419 us
    dot_general x1 -> x8, matrix products: 13.5 us -> 53.3 us  [body(): jnp.einsum('mdr,mdc->rmc', own_block, lax.dynamic_slice_in_dim(grads, sta...]
    all_gather x1 -> x0, waiting for transfers between devices: 27.2 us -> none  [body(): lax.all_gather(basis_rows, 'rep', axis=1, tiled=True)]
    unnamed x5 -> x13, local copies, waits for them, and re-layouts: 82.4 us -> 82.4 us
    unnamed x3 -> x4, other arithmetic: 94.1 us -> 94.1 us
  transfers between devices with their start and end apart: 4 -> 10, of which waited for: 4 -> 3; matrix products, arithmetic and copies ran while one was open for 0% -> 4% of each run, Pallas kernels for 0% -> 0%
where the time goes in v1:
time: 896 us; the launch traced here: 889 us
  waiting for transfers between devices  419 us (47%)
  other arithmetic  216 us (24%)
  local copies, waits for them, and re-layouts  116 us (13%)
  matrix products  106 us (12%)
  between operations  17.2 us (2%)
  starting transfers between devices  14.2 us (2%)
    all_to_all x1, waiting for transfers between devices, body(): lax.all_to_all(grads, 'rep', split_axis=1, concat_axis=2, tiled=True)  161 us
    psum x1, waiting for transfers between devices, body(): gram = lax.psum(local_gram, ('shard', 'rep'))  130 us
    reduce_scatter x1, waiting for transfers between devices, body(): lax.psum_scatter(partial_sum, 'shard', scatter_dimension=0, tiled=True)  128 us
    unnamed x4, other arithmetic  94.1 us
    unnamed x13, local copies, waits for them, and re-layouts  82.4 us
    another operation x14, other arithmetic, body(): factor = jnp.linalg.cholesky(gram)  79 us
    dot_general x8, matrix products, body(): jnp.einsum('mdr,mdc->rmc', own_block, lax.dynamic_slice_in_dim(grads, sta...  53.3 us
    dot_general x8, matrix products, add_block(): jnp.einsum('mdc,mcr->dmr', piece, table, preferred_element_type=jnp.float32)  42.5 us
  transfers between devices with their start and end apart: 10, of which 3 were waited for; matrix products, arithmetic and copies ran while one was open for 4% of the time, Pallas kernels for 0%

profile of v1, /device:TPU:0, one launch (start us, length us, event | category | flops | bytes accessed | tf_op | source)
XLA Modules:
  0.0 889.2 jit_solution(9244973140419626616)
XLA Ops:
  6.5 26.0 %copy.35 = bf16[1,2048,3584]{2,0,1:T(2,128)(2,1)} copy(bf16[1,2048,3584]{2,1,0:T(8,128)(2,1)} %param.4) | data formatting | bytes 29360128 | tf_op args[0]
  33.1 94.1 %reduce.36 = bf16[2048,3584]{1,0:T(8,128)(2,1)} reduce(bf16[2048,1,3584]{2,1,0:T(2,128)(2,1)} %bitcast.244, bf16[]{:T(256)} %broadcast.509), dimensions={1}, to_apply=%bitcast.229.reduce_sub_computation | reduce | bytes 29360130
  127.2 16.2 %reshape.534 = bf16[8,2,458752]{2,1,0:T(2,128)(2,1)} reshape(bf16[2048,3584]{1,0:T(8,128)(2,1)} %reduce.36) | data formatting | bytes 29360128
  143.5 5.6 all-to-all-start
  149.9 161.3 %all-to-all-done = bf16[8,2,458752]{2,1,0:T(2,128)(2,1)} async-done(((bf16[8,2,458752]{2,1,0:T(2,128)(2,1)}), bf16[8,2,458752]{2,1,0:T(2,128)(2,1)}, u32[]{:S(2)}, u32[]{:S(2)}) %all-to-all-start) | async-done | bytes 14680096 | tf_op jit(solution)/shard_map/all_to_all | solution.py:43
  311.2 20.2 %reshape.535 = bf16[2048,1,3584]{2,1,0:T(2,128)(2,1)} reshape(bf16[8,2,458752]{2,1,0:T(2,128)(2,1)} %all-to-all-done) | data formatting | bytes 29360128
  331.4 19.4 %copy.33 = bf16[1,2048,3584]{2,1,0:T(8,128)(2,1)} copy(bf16[1,2048,3584]{2,0,1:T(2,128)(2,1)} %bitcast.245) | data formatting | bytes 29360128
  350.8 18.7 %copy.25 = bf16[1,256,8,3584]{1,3,2,0:T(8,128)(2,1)} copy(bf16[1,256,8,3584]{3,1,2,0:T(8,128)(2,1)} %bitcast.246) | data formatting | bytes 29360128 | tf_op jit(solution)/shard_map/all_to_all | solution.py:43
  369.5 42.8 %while.18 = (s32[]{:T(128)}, f32[256,1,512]{0,2,1:T(8,128)S(1)}, s32[1]{0:T(128)}, bf16[1,256,28672]{1,2,0:T(8,128)(2,1)}, s32[]{:T(128)}, /*index=5*/s32[]{:T(128)}, s32[]{:T(128)}, s32[]{:T(128)}) while((s32[]{:T(128)}, f32[256,1,512]{0,2,1:T(8,128)S(1)}, s32[1]{0:T(128)}, bf16[1,256,28672]{1,2,0:T(8,128)(2,1)}, s32[]{:T(128)}, ...), condition=%wide.region_1.0_spmd.clone, body=%wide.region_0.0_spmd.clone.sunk | while | flops 963648512 | bytes 2912925 | solution.py:52
  374.8 5.3 fusion.119
  415.8 129.5 %all-reduce.3.cloned.1.call-done = f32[1,512,512]{1,2,0:T(8,128)} async-done(((f32[1,512,512]{1,2,0:T(8,128)}), f32[1,512,512]{1,2,0:T(8,128)}) %all-reduce.3.cloned.1.call-update) | async-done | bytes 1048592 | tf_op jit(solution)/shard_map/psum | solution.py:62
  548.4 11.7 %custom-call.34 = f32[1,128,128]{2,1,0:T(8,128)S(1)} custom-call(f32[1,128,128]{2,1,0:T(8,128)S(1)} %cholesky.267), custom_call_target="Cholesky" | custom-call | tf_op jit(solution)/shard_map/jit(cholesky)/cholesky | solution.py:63
  560.1 9.8 %custom-call.35 = f32[1,1,128,128]{2,3,1,0:T(8,128)S(1)} custom-call(f32[1,1,128,128]{3,2,1,0:T(8,128)S(1)} %get-tuple-element.179), custom_call_target="InvertDiagBlocksLowerTriangular" | custom-call | tf_op jit(solution)/shard_map/jit(cholesky)/cholesky | solution.py:63
  570.7 11.7 %custom-call.36 = f32[1,128,128]{2,1,0:T(8,128)S(1)} custom-call(f32[1,128,128]{2,1,0:T(8,128)S(1)} %cholesky.271), custom_call_target="Cholesky" | custom-call | tf_op jit(solution)/shard_map/jit(cholesky)/cholesky | solution.py:63
  582.5 10.2 %custom-call.37 = f32[1,1,128,128]{2,3,1,0:T(8,128)S(1)} custom-call(f32[1,1,128,128]{3,2,1,0:T(8,128)S(1)} %get-tuple-element.176), custom_call_target="InvertDiagBlocksLowerTriangular" | custom-call | tf_op jit(solution)/shard_map/jit(cholesky)/cholesky | solution.py:63
  593.4 11.7 %custom-call.38 = f32[1,128,128]{2,1,0:T(8,128)S(1)} custom-call(f32[1,128,128]{2,1,0:T(8,128)S(1)} %cholesky.276), custom_call_target="Cholesky" | custom-call | tf_op jit(solution)/shard_map/jit(cholesky)/cholesky | solution.py:63
  605.8 9.8 %custom-call.39 = f32[1,1,128,128]{2,3,1,0:T(8,128)S(1)} custom-call(f32[1,1,128,128]{3,2,1,0:T(8,128)S(1)} %get-tuple-element.173), custom_call_target="InvertDiagBlocksLowerTriangular" | custom-call | tf_op jit(solution)/shard_map/jit(cholesky)/cholesky | solution.py:63
  616.2 11.9 %custom-call.40 = f32[1,128,128]{2,1,0:T(8,128)S(1)} custom-call(f32[1,128,128]{2,1,0:T(8,128)S(1)} %fusion.62), custom_call_target="Cholesky" | custom-call | tf_op jit(solution)/shard_map/jit(cholesky)/cholesky | solution.py:63
  632.0 10.5 %while.17 = (s32[]{:T(128)}, f32[1,512,512]{2,1,0:T(8,128)S(1)}, s32[4,2]{0,1:T(2,128)S(1)}, f32[4,1,128,128]{3,2,1,0:T(8,128)}, s32[]{:T(128)}) while((s32[]{:T(128)}, f32[1,512,512]{2,1,0:T(8,128)S(1)}, s32[4,2]{0,1:T(2,128)S(1)}, f32[4,1,128,128]{3,2,1,0:T(8,128)}, s32[]{:T(128)}) %tuple.72), condition=%wide.while_cond, body=%wide.while_body.sunk | while | flops 2 | bytes 132205 | solution.py:65
  642.5 40.1 %custom-call.41 = f32[1,4,128,128]{2,3,1,0:T(8,128)S(1)} custom-call(f32[1,4,128,128]{3,2,1,0:T(8,128)} %bitcast.261), custom_call_target="InvertDiagBlocksLowerTriangular" | custom-call | tf_op jit(solution)/shard_map/triangular_solve | solution.py:65
  692.1 5.8 fusion.42
  700.6 5.7 fusion.40
  729.9 21.0 %add_bitcast_fusion = f32[512,1,3584]{0,2,1:T(8,128)} fusion(f32[3584,512]{1,0:T(8,128)} %fusion.30, f32[3584,512]{1,0:T(8,128)} %fusion.32, f32[3584,512]{1,0:T(8,128)} %fusion.34, f32[3584,512]{1,0:T(8,128)} %fusion.36, f32[3584,512]{1,0:T(8,128)} %fusion.38, f32[3584,512]{1,0:T(8,128)} %fusion.42, f32[3584,512]{1,0:T(8,128)} %fusion.40, ...), kind=kOutput, calls=%fused_computation.25 | convolution fusion | flops 952369152 | bytes 60817412 | tf_op jit(solution)/shard_map/mdr,mdc->rmc/dot_general | solution.py:72
  751.0 128.3 %reduce-scatter.2.cloned.1.call-done = f32[128,1,3584]{0,2,1:T(8,128)} async-done(((f32[512,1,3584]{0,2,1:T(8,128)}), f32[128,1,3584]{0,2,1:T(8,128)}) %reduce-scatter.2.cloned.1.call-update) | async-done | bytes 1835024 | tf_op jit(solution)/shard_map/reduce_scatter | solution.py:79
  (96 shorter events, 97.7 us)
Async XLA Ops:
  143.5 167.7 %all-to-all-start = ((bf16[8,2,458752]{2,1,0:T(2,128)(2,1)}), bf16[8,2,458752]{2,1,0:T(2,128)(2,1)}, u32[]{:S(2)}, u32[]{:S(2)}) async-start(bf16[8,2,458752]{2,1,0:T(2,128)(2,1)} %reshape.534), calls=%async_computation | async-start | bytes 29360128 | tf_op jit(solution)/shard_map/all_to_all | solution.py:43
  149.0 396.3 %all-reduce.3.cloned.1.call-start = ((), (), s32[]{:S(2)}) async-start(), calls=%async_computation.2 | async-start | bytes 2097152 | tf_op jit(solution)/shard_map/psum | solution.py:62
  414.4 464.9 %reduce-scatter.2.cloned.1.call-start = ((), (), s32[]{:S(2)}) async-start(), calls=%async_computation.3 | async-start | bytes 9175040 | tf_op jit(solution)/shard_map/reduce_scatter | solution.py:79
  632.0 74.2 %slice-start = ((s8[14680064]{0:T(1024)(128)(4,1)}), s8[2097152]{0:T(1024)(128)(4,1)S(1)}, s32[]{:S(2)}) async-start(s8[14680064]{0:T(1024)(128)(4,1)} %bitcast.247), calls=%async_computation.4 | async-start | bytes 4194304
  689.4 8.5 collective-permute-start.1
  689.5 8.4 collective-permute-start
  692.1 14.1 %slice-start.1 = ((s8[14680064]{0:T(1024)(128)(4,1)}), s8[4194304]{0:T(1024)(128)(4,1)S(1)}, s32[]{:S(2)}) async-start(s8[14680064]{0:T(1024)(128)(4,1)} %bitcast.247), calls=%async_computation.5 | async-start | bytes 8388608
  692.1 14.1 %slice-start.2 = ((s8[14680064]{0:T(1024)(128)(4,1)}), s8[4194304]{0:T(1024)(128)(4,1)S(1)}, s32[]{:S(2)}) async-start(s8[14680064]{0:T(1024)(128)(4,1)} %bitcast.247), calls=%async_computation.6 | async-start | bytes 8388608
  697.9 8.3 slice-start.3
  697.9 12.4 %collective-permute-start.3 = (bf16[1,256,512]{1,2,0:T(8,128)(2,1)S(1)}, bf16[1,256,512]{1,2,0:T(8,128)(2,1)S(1)}, u32[]{:S(2)}, u32[]{:S(2)}) collective-permute-start(bf16[1,256,512]{1,2,0:T(8,128)(2,1)S(1)} %collective-permute-done.1), channel_id=1, source_target_pairs={{0,1},{1,2},{2,3},{3,4},{4,5},{5,6},{6,7},{7,0},{8,9},{9,10},{10,1... | collective-permute-start | bytes 786440 | tf_op jit(solution)/shard_map/ppermute | solution.py:20
  697.9 12.4 %collective-permute-start.2 = (bf16[1,256,512]{1,2,0:T(8,128)(2,1)S(1)}, bf16[1,256,512]{1,2,0:T(8,128)(2,1)S(1)}, u32[]{:S(2)}, u32[]{:S(2)}) collective-permute-start(bf16[1,256,512]{1,2,0:T(8,128)(2,1)S(1)} %collective-permute-done), channel_id=1, source_target_pairs={{0,7},{1,0},{2,1},{3,2},{4,3},{5,4},{6,5},{7,6},{8,15},{9,8},{10,9... | collective-permute-start | bytes 786440 | tf_op jit(solution)/shard_map/ppermute | solution.py:22
  710.4 11.0 %collective-permute-start.5 = (bf16[1,256,512]{1,2,0:T(8,128)(2,1)S(1)}, bf16[1,256,512]{1,2,0:T(8,128)(2,1)S(1)}, u32[]{:S(2)}, u32[]{:S(2)}) collective-permute-start(bf16[1,256,512]{1,2,0:T(8,128)(2,1)S(1)} %collective-permute-done.3), channel_id=1, source_target_pairs={{0,1},{1,2},{2,3},{3,4},{4,5},{5,6},{6,7},{7,0},{8,9},{9,10},{10,1... | collective-permute-start | bytes 786440 | tf_op jit(solution)/shard_map/ppermute | solution.py:20
  710.4 15.3 %collective-permute-start.4 = (bf16[1,256,512]{1,2,0:T(8,128)(2,1)S(1)}, bf16[1,256,512]{1,2,0:T(8,128)(2,1)S(1)}, u32[]{:S(2)}, u32[]{:S(2)}) collective-permute-start(bf16[1,256,512]{1,2,0:T(8,128)(2,1)S(1)} %collective-permute-done.2), channel_id=1, source_target_pairs={{0,7},{1,0},{2,1},{3,2},{4,3},{5,4},{6,5},{7,6},{8,15},{9,8},{10,9... | collective-permute-start | bytes 786440 | tf_op jit(solution)/shard_map/ppermute | solution.py:22
  721.3 8.6 collective-permute-start.6
Sparse Core Ops, SparseCore 0:
  414.5 130.7 all-reduce.2
  751.1 128.1 reduce-scatter.1
